TPU v7x, 32 devices: a whole 2x2x4 slice. The times are simulated.
32 devices in a mesh: groups: 2 (over y), space: 16 (over z, x, core).
Axes of the slice: x: 2, y: 2, z: 4, core: 2. Of those that a mesh axis runs over, the one named last changes fastest.
Arguments:
- field: float32 [64, 40, 8, 256], P(('groups', 'space')), parts along dimension 0, may hold values from -6 to 6
- grad_out: float32 [64, 40, 8, 256], P(('groups', 'space')), parts along dimension 0, may hold values from -6 to 6
- weight: float32 [256, 27, 256], P('space'), may hold values from -0.078125 to 0.078125
- bias: float32 [256], replicated, may hold values from -3 to 3
- land_bias: float32 [256], replicated, may hold values from -3 to 3
- level_gain: float32 [4, 256], replicated, may hold values from 0.5 to 1.5
- land_mask: int32 [32, 40], P('space'), may hold values 0 or 1
- level_index: int32 [8], replicated, may hold values from 0 to 3, as said below
Outputs:
- grad_field: float32 [64, 40, 8, 256], P(('groups', 'space')), parts along dimension 0
- grad_weight: float32 [512, 27, 256], P(('groups', 'space')), parts along dimension 0
- grad_bias: float32 [512], P('groups'), parts along dimension 0
- grad_land: float32 [512], P('groups'), parts along dimension 0
- grad_gain: float32 [8, 256], P('groups'), parts along dimension 0
There are 2 independent parts, one for each index of `groups`. A program takes and returns all parts, laid end to end along the dimension named above; an argument that names none is the same for every part. Nothing has to cross between parts.
Inputs may be any that keep to these rules, and one draw needn't show every extreme that they name: `level_index`: a gain table row for each level; every row of the table is used by some level.
All inputs are finite; a program needn't handle non-finite values. No bound on the sum of `land_mask` on one device may be relied on, other than what follows from the above.
Results may differ from a plain program's by a relative error of at most 0.00011.
Values sent between devices are 32-bit elements; how exact they have to be, the bound alone decides.
No kernel may reach another device: no remote copies, remote signals or barrier semaphores. Data moves between devices by JAX's collectives and lax.ppermute only.
A program may use at most 128 MiB of HBM per device.

v0:
```python
import jax
import jax.numpy as jnp
from jax import lax
from jax.sharding import PartitionSpec as P

highest = lax.Precision.HIGHEST
high = lax.Precision.HIGH


def with_halo(array, sides, width):
    for axis, dim in sides:
        count, length = (lax.axis_size(axis), array.shape[dim])
        up = [(i, (i + 1) % count) for i in range(count - 1)]
        down = [(j, i) for i, j in up]
        last = lax.slice_in_dim(array, length - width, length, axis=dim)
        leading = lax.slice_in_dim(array, 0, width, axis=dim)
        before = lax.ppermute(last, axis, up)
        after = lax.ppermute(leading, axis, down)
        array = jnp.concatenate([before, array, after], axis=dim)
    return array


def wrap_levels(field):
    wrapped = jnp.concatenate([field[:, -1:], field, field[:, :1]], axis=1)
    return jnp.pad(wrapped, ((0, 0), (0, 0), (1, 1), (0, 0)))


def window_table(grid, out_rows, flipped):
    lon_n = grid.shape[1] - 2
    lev_n = grid.shape[2] - 2
    chans = grid.shape[3]
    windows = []
    for offset in range(27):
        lat_off, remainder = divmod(offset, 9)
        lon_off, lev_off = divmod(remainder, 3)
        if flipped:
            lat_off, lon_off, lev_off = (2 - lat_off, 2 - lon_off, 2 - lev_off)
        window = grid[
            lat_off : lat_off + out_rows, lon_off : lon_off + lon_n, lev_off : lev_off + lev_n
        ]
        windows.append(window.reshape(-1, chans))
    return jnp.stack(windows, axis=1)


def conv_piece(table, piece):
    return jnp.einsum("rop,poc->rc", table, piece, precision=high)


def back_piece(table, piece):
    return jnp.einsum("roc,qoc->rq", table, piece, precision=high)


def stacked_product(delta_flat, table):
    d_hi, d_lo = split_bf16(delta_flat)
    t_hi, t_lo = split_bf16(table)
    lhs = jnp.concatenate([d_hi, d_hi, d_lo], axis=0)
    rhs = jnp.concatenate([t_hi, t_lo, t_hi], axis=0)
    return jnp.einsum("rq,rop->opq", lhs, rhs, preferred_element_type=jnp.float32)


def all_sum(x):
    count = lax.axis_size("space")
    if count & count - 1:
        return lax.psum(x, "space")
    bit = 1
    while bit < count:
        x = x + lax.ppermute(x, "space", [(i, i ^ bit) for i in range(count)])
        bit *= 2
    return x


def split_bf16(x):
    hi = lax.reduce_precision(x, exponent_bits=8, mantissa_bits=7)
    return (hi.astype(jnp.bfloat16), (x - hi).astype(jnp.bfloat16))


def per_device(field, grad_out, weight, bias, land_bias, level_gain, land_mask, level_index):
    rows, lon_n, lev_n, chans = field.shape
    land_float = land_mask.astype(jnp.float32)
    one_hot = (
        level_index[:, None] == jnp.arange(level_gain.shape[0], dtype=jnp.int32)[None, :]
    ).astype(jnp.float32)
    gains = jnp.dot(one_hot, level_gain, precision=highest)
    full_weight = lax.all_gather(weight, "space", axis=0, tiled=True)
    grid_pre = wrap_levels(with_halo(field, (("space", 0),), 1))
    table_pre = window_table(grid_pre, rows, False)
    conv = conv_piece(table_pre, full_weight)
    conv = conv.reshape(rows, lon_n, lev_n, chans)
    pre = conv + bias + land_float[:, :, None, None] * land_bias
    sigma = jax.nn.sigmoid(pre)
    active = pre * sigma
    delta = grad_out * gains * sigma * (1.0 + pre * (1.0 - sigma))
    delta_pad = with_halo(delta, (("space", 0),), 1)
    delta_table = window_table(wrap_levels(delta_pad), rows, True)
    back = back_piece(delta_table, full_weight)
    grad_field = grad_out + back.reshape(rows, lon_n, lev_n, chans)
    local_bias = jnp.sum(delta, axis=(0, 1, 2))
    local_land = jnp.sum(land_float[:, :, None, None] * delta, axis=(0, 1, 2))
    per_level = jnp.sum(grad_out * active, axis=(0, 1))
    local_gain = jnp.dot(one_hot.T, per_level, precision=highest)
    sums = all_sum(jnp.concatenate([local_bias[None], local_land[None], local_gain], axis=0))
    delta_flat = delta.reshape(-1, chans)
    grad_weight = lax.psum_scatter(
        stacked_product(delta_flat, table_pre), "space", scatter_dimension=1, tiled=True
    )
    grad_weight = jnp.transpose(grad_weight, (1, 0, 2))
    return (grad_field, grad_weight, sums[0], sums[1], sums[2 : 2 + local_gain.shape[0]])


def solution(mesh):
    in_specs = (
        P(("groups", "space"), None, None, None),
        P(("groups", "space"), None, None, None),
        P("space", None, None),
        P(),
        P(),
        P(),
        P("space", None),
        P(),
    )
    out_specs = (
        P(("groups", "space"), None, None, None),
        P(("groups", "space"), None, None),
        P("groups"),
        P("groups"),
        P("groups", None),
    )
    return jax.shard_map(
        per_device, mesh=mesh, in_specs=in_specs, out_specs=out_specs, check_vma=False
    )
```

profile of v0, /device:TPU:0, one launch (start us, length us, event | category | flops | bytes accessed | tf_op | source)
XLA Modules:
  0.0 206.0 jit_solution(803695057500846920)
XLA Ops:
  8.0 1.1 fusion.30
  9.1 1.3 collective-permute-start.1
  10.4 3.1 %collective-permute-start = (f32[1,40,8,256]{3,2,1,0:T(8,128)S(1)}, f32[1,40,8,256]{3,2,1,0:T(8,128)S(1)}, u32[]{:S(2)}, u32[]{:S(2)}) collective-permute-start(f32[1,40,8,256]{3,2,1,0:T(8,128)S(1)} %get-tuple-element.78), channel_id=1, source_target_pairs={{0,1},{1,2},{2,3},{3,4},{4,5},{5,6},{6,7},{7,8},{8,9},{9,10},{10,1... | collective-permute-start | bytes 983048 | tf_op jit(solution)/shard_map/ppermute | solution.py:17
  15.8 2.5 %pad_maximum_fusion.4 = (f32[2,40,8,256]{3,2,1,0:T(8,128)}, f32[4,40,8,256]{3,2,1,0:T(8,128)S(1)}, f32[2,40,8,256]{3,2,1,0:T(8,128)}) fusion(f32[1,40,8,256]{3,2,1,0:T(8,128)S(1)} %collective-permute-done.1, f32[2,40,8,256]{3,2,1,0:T(8,128)} %param.8, f32[4,40,8,256]{3,2,1,0:T(8,128)S(1)} %constant_dynamic-update-slice_fusion.2, ...), kind=kLoop, calls=%fused_computation.43 | loop fusion | flops 327680 | bytes 3276800 | tf_op jit(solution)/shard_map/concatenate | solution.py:19
  18.3 1.1 copy-done.3
  19.8 4.4 %fusion.25 = (f32[2,40,8,256]{3,2,1,0:T(8,128)}, f32[2,40,8,256]{3,2,1,0:T(8,128)}, f32[2,40,8,256]{3,2,1,0:T(8,128)}, f32[2,40,8,256]{3,2,1,0:T(8,128)}, f32[2,...) fusion(f32[4,42,10,256]{3,2,1,0:T(8,128)S(1)} %select_maximum_f, ...), kind=kLoop, calls=%fused_computation.122 | loop fusion | bytes 23592960 | tf_op jit(solution)/shard_map/slice | solution.py:38
  24.4 1.3 constant_dynamic-update-slice_fusion.29
  25.7 3.1 %pad_maximum_fusion.3 = (f32[2,40,8,256]{3,2,1,0:T(8,128)S(1)}, f32[2,40,8,256]{3,2,1,0:T(8,128)S(1)}, f32[2,40,8,256]{3,2,1,0:T(8,128)S(1)}, f32[2,40,8,256]{3,...) fusion(f32[4,1,8,256]{3,2,1,0:T(8,128)} %copy-done.36, f32[4,40,8,256]{3,2,1,0:T(8,128)} %copy-done.3, ...), kind=kLoop, calls=%fused_computation.42 | loop fusion | flops 983040 | bytes 5308416 | tf_op jit(solution)/shard_map/concatenate | solution.py:24
  28.9 1.2 constant_dynamic-update-slice_fusion.27
  30.1 1.1 constant_dynamic-update-slice_fusion.26
  31.2 1.1 constant_dynamic-update-slice_fusion.25
  32.4 1.1 constant_dynamic-update-slice_fusion.24
  33.5 1.1 constant_dynamic-update-slice_fusion.23
  34.7 1.1 constant_dynamic-update-slice_fusion.21
  35.8 1.1 constant_dynamic-update-slice_fusion.20
  38.0 6.6 %copy-done.2 = f32[640,27,256]{2,0,1:T(8,128)} copy-done((f32[640,27,256]{2,0,1:T(8,128)}, f32[640,27,256]{2,0,1:T(8,128)S(1)}, u32[]{:S(2)}) %copy-start.2) | copy-done | bytes 17694744
  44.6 7.4 %fusion.6 = (bf16[640,27,256]{2,0,1:T(8,128)(2,1)}, bf16[640,27,256]{2,0,1:T(8,128)(2,1)}) fusion(f32[640,27,256]{2,0,1:T(8,128)S(1)} %constant_dynamic-update-slice_fusion.3), kind=kLoop, calls=%fused_computation.8 | loop fusion | flops 17694720 | bytes 35389440 | tf_op jit(solution)/shard_map/convert_element_type | solution.py:74
  52.0 27.6 %all-gather.2.cloned.1.call-done = f32[256,27,256]{2,0,1:T(8,128)} async-done(((f32[16,27,256]{2,0,1:T(8,128)}), f32[256,27,256]{2,0,1:T(8,128)}) %all-gather.2.cloned.1.call-update) | async-done | bytes 7077904 | tf_op jit(solution)/shard_map/all_gather | solution.py:84
  79.6 13.7 %fusion.32 = f32[640,256,1]{1,0,2:T(8,128)S(1)} fusion(f32[640,27,256]{2,0,1:T(8,128)} %copy-done.2, f32[256,27,256]{2,0,1:T(8,128)} %all-gather.2.cloned.1.call-done), kind=kOutput, calls=%fused_computation.129 | convolution fusion | flops 6794772480 | bytes 25427968 | tf_op jit(solution)/shard_map/rop,poc->rc/dot_general | solution.py:46
  93.9 16.7 %fusion = f32[27,256,256]{2,1,0:T(8,128)} fusion(bf16[640,27,256]{2,0,1:T(8,128)(2,1)} %get-tuple-element.9, bf16[640,27,256]{2,0,1:T(8,128)(2,1)} %get-tuple-element.8, bf16[640,256]{1,0:T(8,128)(2,1)S(1)} %get-tuple-element.69, bf16[640,256]{1,0:T(8,128)(2,1)S(1)} %get-tuple-element.68), kind=kOutput, calls=%fused_computation | convolution fusion | flops 6877347840 | bytes 25427968 | tf_op jit(solution)/shard_map/rq,rop->opq/dot_general | solution.py:58
  111.3 2.2 %collective-permute-start.2 = (f32[1,40,8,256]{3,2,1,0:T(8,128)S(1)}, f32[1,40,8,256]{3,2,1,0:T(8,128)S(1)}, u32[]{:S(2)}, u32[]{:S(2)}) collective-permute-start(f32[1,40,8,256]{3,2,1,0:T(8,128)S(1)} %get-tuple-element.72), channel_id=1, source_target_pairs={{0,1},{1,2},{2,3},{3,4},{4,5},{5,6},{6,7},{7,8},{8,9},{9,10},{10,1... | collective-permute-start | bytes 983048 | tf_op jit(solution)/shard_map/ppermute | solution.py:17
  113.5 1.5 collective-permute-start.3
  115.0 2.7 %collective-permute-start.5 = (f32[6,256]{1,0:T(8,128)S(1)}, f32[6,256]{1,0:T(8,128)S(1)}, u32[]{:S(2)}, u32[]{:S(2)}) collective-permute-start(f32[6,256]{1,0:T(8,128)S(1)} %fusion.22), channel_id=1, source_target_pairs={{0,2},{1,3},{2,0},{3,1},{4,6},{5,7},{6,4},{7,5},{8,10},{9,11},{10,... | collective-permute-start | bytes 18440 | tf_op jit(solution)/shard_map/ppermute | solution.py:67
  117.7 4.9 %collective-permute-done.5 = f32[6,256]{1,0:T(8,128)S(1)} collective-permute-done((f32[6,256]{1,0:T(8,128)S(1)}, f32[6,256]{1,0:T(8,128)S(1)}, u32[]{:S(2)}, u32[]{:S(2)}) %collective-permute-start.5) | collective-permute-done | bytes 6176 | tf_op jit(solution)/shard_map/ppermute | solution.py:67
  122.6 2.9 %collective-permute-start.6 = (f32[6,256]{1,0:T(8,128)S(1)}, f32[6,256]{1,0:T(8,128)S(1)}, u32[]{:S(2)}, u32[]{:S(2)}) collective-permute-start(f32[6,256]{1,0:T(8,128)S(1)} %add.51), channel_id=1, source_target_pairs={{0,4},{1,5},{2,6},{3,7},{4,0},{5,1},{6,2},{7,3},{8,12},{9,13},{10,... | collective-permute-start | bytes 18440 | tf_op jit(solution)/shard_map/ppermute | solution.py:67
  125.5 1.6 collective-permute-done.6
  127.2 2.5 %collective-permute-start.7 = (f32[6,256]{1,0:T(8,128)S(1)}, f32[6,256]{1,0:T(8,128)S(1)}, u32[]{:S(2)}, u32[]{:S(2)}) collective-permute-start(f32[6,256]{1,0:T(8,128)S(1)} %add.52), channel_id=1, source_target_pairs={{0,8},{1,9},{2,10},{3,11},{4,12},{5,13},{6,14},{7,15},{8,0},{9,1},... | collective-permute-start | bytes 18440 | tf_op jit(solution)/shard_map/ppermute | solution.py:67
  129.7 2.0 collective-permute-done.7
  134.4 4.4 %fusion.24 = (f32[2,40,8,256]{3,2,1,0:T(8,128)}, f32[2,40,8,256]{3,2,1,0:T(8,128)}, f32[2,40,8,256]{3,2,1,0:T(8,128)}, f32[2,40,8,256]{3,2,1,0:T(8,128)}, f32[2,...) fusion(f32[4,42,10,256]{3,2,1,0:T(8,128)S(1)} %select_maximum_f, ...), kind=kLoop, calls=%fused_computation.121 | loop fusion | bytes 23592960 | tf_op jit(solution)/shard_map/slice | solution.py:38
  138.9 2.3 %constant_dynamic-update-slice_fusion.56 = f32[640,27,256]{2,0,1:T(8,128)} fusion(f32[640,1,256]{2,0,1:T(8,128)} %bitcast.118), kind=kLoop, calls=%fused_computation.107 | loop fusion | bytes 1310720
  141.1 1.9 maximum_maximum_fusion
  144.4 2.1 %constant_dynamic-update-slice_fusion.54 = f32[640,27,256]{2,0,1:T(8,128)} fusion(f32[640,27,256]{2,0,1:T(8,128)} %constant_dynamic-update-slice_fusion.55, f32[640,1,256]{2,0,1:T(8,128)} %bitcast.114), kind=kLoop, calls=%fused_computation.105 | loop fusion | bytes 1310720
  146.5 2.0 constant_dynamic-update-slice_fusion.53
  148.5 1.2 pad_maximum_fusion.1
  152.4 0.9 constant_dynamic-update-slice_fusion.49
  153.3 0.9 constant_dynamic-update-slice_fusion.48
  155.1 0.9 constant_dynamic-update-slice_fusion.46
  156.0 1.0 constant_dynamic-update-slice_fusion.45
  157.0 1.0 constant_dynamic-update-slice_fusion.44
  158.8 0.9 constant_dynamic-update-slice_fusion.42
  162.4 0.9 constant_dynamic-update-slice_fusion.38
  166.0 0.9 constant_dynamic-update-slice_fusion.34
  166.9 0.9 constant_dynamic-update-slice_fusion.33
  168.7 0.9 constant_dynamic-update-slice_fusion.31
  169.6 0.9 constant_dynamic-update-slice_fusion.30
  170.5 10.7 %fusion.33 = f32[640,256,1]{1,0,2:T(8,128)S(1)} fusion(f32[640,27,256]{2,0,1:T(8,128)} %constant_dynamic-update-slice_fusion.30, f32[256,27,256]{2,0,1:T(8,128)S(1)} %bitcast.79), kind=kOutput, calls=%fused_computation.130 | convolution fusion | flops 6794772480 | bytes 25427968 | tf_op jit(solution)/shard_map/roc,qoc->rq/dot_general | solution.py:50
  181.2 0.9 add.49
  182.1 17.1 %reduce-scatter.2.cloned.1.call-done = f32[27,16,256]{2,1,0:T(8,128)} async-done(((f32[27,256,256]{2,1,0:T(8,128)}), f32[27,16,256]{2,1,0:T(8,128)}) %reduce-scatter.2.cloned.1.call-update) | async-done | bytes 442384 | tf_op jit(solution)/shard_map/reduce_scatter | solution.py:103
  (144 shorter events, 20.3 us)
Async XLA Ops:
  7.2 7.7 %copy-start = (f32[4,256]{1,0:T(4,128)S(1)}, f32[4,256]{1,0:T(4,128)}, u32[]{:S(2)}) copy-start(f32[4,256]{1,0:T(4,128)} %param.13) | copy-start | bytes 12292
  7.2 72.4 %all-gather.2.cloned.1.call-start = ((), (), s32[]{:S(2)}) async-start(), calls=%async_computation.1 | async-start | bytes 7520256 | tf_op jit(solution)/shard_map/all_gather | solution.py:84
  7.9 191.2 %reduce-scatter.2.cloned.1.call-start = ((), (), s32[]{:S(2)}) async-start(), calls=%async_computation.2 | async-start | bytes 7520256 | tf_op jit(solution)/shard_map/reduce_scatter | solution.py:103
  9.1 6.7 %collective-permute-start.1 = (f32[1,40,8,256]{3,2,1,0:T(8,128)S(1)}, f32[1,40,8,256]{3,2,1,0:T(8,128)S(1)}, u32[]{:S(2)}, u32[]{:S(2)}) collective-permute-start(f32[1,40,8,256]{3,2,1,0:T(8,128)S(1)} %get-tuple-element.77), channel_id=1, source_target_pairs={{1,0},{2,1},{3,2},{4,3},{5,4},{6,5},{7,6},{8,7},{9,8},{10,9},{11,1... | collective-permute-start | bytes 983048 | tf_op jit(solution)/shard_map/ppermute | solution.py:18
  10.4 5.4 %collective-permute-start = (f32[1,40,8,256]{3,2,1,0:T(8,128)S(1)}, f32[1,40,8,256]{3,2,1,0:T(8,128)S(1)}, u32[]{:S(2)}, u32[]{:S(2)}) collective-permute-start(f32[1,40,8,256]{3,2,1,0:T(8,128)S(1)} %get-tuple-element.78), channel_id=1, source_target_pairs={{0,1},{1,2},{2,3},{3,4},{4,5},{5,6},{6,7},{7,8},{8,9},{9,10},{10,1... | collective-permute-start | bytes 983048 | tf_op jit(solution)/shard_map/ppermute | solution.py:17
  18.3 1.1 copy-start.3
  19.8 17.3 %copy-start.4 = (f32[2,40,8,256]{3,2,1,0:T(8,128)S(1)}, f32[2,40,8,256]{3,2,1,0:T(8,128)}, u32[]{:S(2)}) copy-start(f32[2,40,8,256]{3,2,1,0:T(8,128)} %param.8) | copy-start | bytes 1966084
  24.3 12.7 %copy-start.30 = (f32[2,40,8,256]{3,2,1,0:T(8,128)S(1)}, f32[2,40,8,256]{3,2,1,0:T(8,128)}, u32[]{:S(2)}) copy-start(f32[2,40,8,256]{3,2,1,0:T(8,128)} %get-tuple-element.38) | copy-start | bytes 1966084
  24.3 12.8 %copy-start.29 = (f32[2,40,8,256]{3,2,1,0:T(8,128)S(1)}, f32[2,40,8,256]{3,2,1,0:T(8,128)}, u32[]{:S(2)}) copy-start(f32[2,40,8,256]{3,2,1,0:T(8,128)} %get-tuple-element.37) | copy-start | bytes 1966084
  24.3 12.9 %copy-start.26 = (f32[2,40,8,256]{3,2,1,0:T(8,128)S(1)}, f32[2,40,8,256]{3,2,1,0:T(8,128)}, u32[]{:S(2)}) copy-start(f32[2,40,8,256]{3,2,1,0:T(8,128)} %get-tuple-element.36) | copy-start | bytes 1966084
  24.3 13.0 %copy-start.25 = (f32[2,40,8,256]{3,2,1,0:T(8,128)S(1)}, f32[2,40,8,256]{3,2,1,0:T(8,128)}, u32[]{:S(2)}) copy-start(f32[2,40,8,256]{3,2,1,0:T(8,128)} %get-tuple-element.35) | copy-start | bytes 1966084
  24.3 13.1 %copy-start.22 = (f32[2,40,8,256]{3,2,1,0:T(8,128)S(1)}, f32[2,40,8,256]{3,2,1,0:T(8,128)}, u32[]{:S(2)}) copy-start(f32[2,40,8,256]{3,2,1,0:T(8,128)} %get-tuple-element.34) | copy-start | bytes 1966084
  24.3 13.1 %copy-start.21 = (f32[2,40,8,256]{3,2,1,0:T(8,128)S(1)}, f32[2,40,8,256]{3,2,1,0:T(8,128)}, u32[]{:S(2)}) copy-start(f32[2,40,8,256]{3,2,1,0:T(8,128)} %get-tuple-element.33) | copy-start | bytes 1966084
  24.3 13.2 %copy-start.18 = (f32[2,40,8,256]{3,2,1,0:T(8,128)S(1)}, f32[2,40,8,256]{3,2,1,0:T(8,128)}, u32[]{:S(2)}) copy-start(f32[2,40,8,256]{3,2,1,0:T(8,128)} %get-tuple-element.32) | copy-start | bytes 1966084
  24.4 13.3 %copy-start.17 = (f32[2,40,8,256]{3,2,1,0:T(8,128)S(1)}, f32[2,40,8,256]{3,2,1,0:T(8,128)}, u32[]{:S(2)}) copy-start(f32[2,40,8,256]{3,2,1,0:T(8,128)} %get-tuple-element.31) | copy-start | bytes 1966084
  24.4 13.3 %copy-start.35 = (f32[2,40,8,256]{3,2,1,0:T(8,128)S(1)}, f32[2,40,8,256]{3,2,1,0:T(8,128)}, u32[]{:S(2)}) copy-start(f32[2,40,8,256]{3,2,1,0:T(8,128)} %get-tuple-element.74) | copy-start | bytes 1966084
  24.4 13.4 %copy-start.14 = (f32[2,40,8,256]{3,2,1,0:T(8,128)S(1)}, f32[2,40,8,256]{3,2,1,0:T(8,128)}, u32[]{:S(2)}) copy-start(f32[2,40,8,256]{3,2,1,0:T(8,128)} %get-tuple-element.30) | copy-start | bytes 1966084
  25.7 12.2 %copy-start.13 = (f32[2,40,8,256]{3,2,1,0:T(8,128)S(1)}, f32[2,40,8,256]{3,2,1,0:T(8,128)}, u32[]{:S(2)}) copy-start(f32[2,40,8,256]{3,2,1,0:T(8,128)} %get-tuple-element.29) | copy-start | bytes 1966084
  28.8 9.1 %copy-start.10 = (f32[2,40,8,256]{3,2,1,0:T(8,128)S(1)}, f32[2,40,8,256]{3,2,1,0:T(8,128)}, u32[]{:S(2)}) copy-start(f32[2,40,8,256]{3,2,1,0:T(8,128)} %get-tuple-element.28) | copy-start | bytes 1966084
  38.0 6.6 %copy-start.2 = (f32[640,27,256]{2,0,1:T(8,128)}, f32[640,27,256]{2,0,1:T(8,128)S(1)}, u32[]{:S(2)}) copy-start(f32[640,27,256]{2,0,1:T(8,128)S(1)} %constant_dynamic-update-slice_fusion.3) | copy-start | bytes 53084164
  52.0 41.4 %copy-start.33 = (f32[2,40,8,256]{3,2,1,0:T(8,128)S(1)}, f32[2,40,8,256]{3,2,1,0:T(8,128)}, u32[]{:S(2)}) copy-start(f32[2,40,8,256]{3,2,1,0:T(8,128)} %param.9) | copy-start | bytes 1966084
  52.0 41.4 %copy-start.37 = (f32[256]{0:T(256)S(1)}, f32[256]{0:T(256)}, u32[]{:S(2)}) copy-start(f32[256]{0:T(256)} %param.11) | copy-start | bytes 3076
  93.9 16.8 %copy-start.38 = (s32[8]{0:T(128)S(1)}, s32[8]{0:T(128)}, u32[]{:S(2)}) copy-start(s32[8]{0:T(128)} %param.15) | copy-start | bytes 100
  110.9 4.0 %collective-permute-start.4 = (f32[6,256]{1,0:T(8,128)S(1)}, f32[6,256]{1,0:T(8,128)S(1)}, u32[]{:S(2)}, u32[]{:S(2)}) collective-permute-start(f32[6,256]{1,0:T(8,128)S(1)} %pad_maximum_fusion.10), channel_id=1, source_target_pairs={{0,1},{1,0},{2,3},{3,2},{4,5},{5,4},{6,7},{7,6},{8,9},{9,8},{10,11... | collective-permute-start | bytes 18440 | tf_op jit(solution)/shard_map/ppermute | solution.py:67
  111.3 21.6 %collective-permute-start.2 = (f32[1,40,8,256]{3,2,1,0:T(8,128)S(1)}, f32[1,40,8,256]{3,2,1,0:T(8,128)S(1)}, u32[]{:S(2)}, u32[]{:S(2)}) collective-permute-start(f32[1,40,8,256]{3,2,1,0:T(8,128)S(1)} %get-tuple-element.72), channel_id=1, source_target_pairs={{0,1},{1,2},{2,3},{3,4},{4,5},{5,6},{6,7},{7,8},{8,9},{9,10},{10,1... | collective-permute-start | bytes 983048 | tf_op jit(solution)/shard_map/ppermute | solution.py:17
  113.5 19.4 %collective-permute-start.3 = (f32[1,40,8,256]{3,2,1,0:T(8,128)S(1)}, f32[1,40,8,256]{3,2,1,0:T(8,128)S(1)}, u32[]{:S(2)}, u32[]{:S(2)}) collective-permute-start(f32[1,40,8,256]{3,2,1,0:T(8,128)S(1)} %get-tuple-element.73), channel_id=1, source_target_pairs={{1,0},{2,1},{3,2},{4,3},{5,4},{6,5},{7,6},{8,7},{9,8},{10,9},{11,1... | collective-permute-start | bytes 983048 | tf_op jit(solution)/shard_map/ppermute | solution.py:18
  115.0 7.6 %collective-permute-start.5 = (f32[6,256]{1,0:T(8,128)S(1)}, f32[6,256]{1,0:T(8,128)S(1)}, u32[]{:S(2)}, u32[]{:S(2)}) collective-permute-start(f32[6,256]{1,0:T(8,128)S(1)} %fusion.22), channel_id=1, source_target_pairs={{0,2},{1,3},{2,0},{3,1},{4,6},{5,7},{6,4},{7,5},{8,10},{9,11},{10,... | collective-permute-start | bytes 18440 | tf_op jit(solution)/shard_map/ppermute | solution.py:67
  122.6 4.5 %collective-permute-start.6 = (f32[6,256]{1,0:T(8,128)S(1)}, f32[6,256]{1,0:T(8,128)S(1)}, u32[]{:S(2)}, u32[]{:S(2)}) collective-permute-start(f32[6,256]{1,0:T(8,128)S(1)} %add.51), channel_id=1, source_target_pairs={{0,4},{1,5},{2,6},{3,7},{4,0},{5,1},{6,2},{7,3},{8,12},{9,13},{10,... | collective-permute-start | bytes 18440 | tf_op jit(solution)/shard_map/ppermute | solution.py:67
  127.2 4.5 %collective-permute-start.7 = (f32[6,256]{1,0:T(8,128)S(1)}, f32[6,256]{1,0:T(8,128)S(1)}, u32[]{:S(2)}, u32[]{:S(2)}) collective-permute-start(f32[6,256]{1,0:T(8,128)S(1)} %add.52), channel_id=1, source_target_pairs={{0,8},{1,9},{2,10},{3,11},{4,12},{5,13},{6,14},{7,15},{8,0},{9,1},... | collective-permute-start | bytes 18440 | tf_op jit(solution)/shard_map/ppermute | solution.py:67
  138.8 11.8 %copy-start.32 = (f32[2,40,8,256]{3,2,1,0:T(8,128)S(1)}, f32[2,40,8,256]{3,2,1,0:T(8,128)}, u32[]{:S(2)}) copy-start(f32[2,40,8,256]{3,2,1,0:T(8,128)} %get-tuple-element.24) | copy-start | bytes 1966084
  138.8 12.7 %copy-start.31 = (f32[2,40,8,256]{3,2,1,0:T(8,128)S(1)}, f32[2,40,8,256]{3,2,1,0:T(8,128)}, u32[]{:S(2)}) copy-start(f32[2,40,8,256]{3,2,1,0:T(8,128)} %get-tuple-element.23) | copy-start | bytes 1966084
  138.8 14.5 %copy-start.28 = (f32[2,40,8,256]{3,2,1,0:T(8,128)S(1)}, f32[2,40,8,256]{3,2,1,0:T(8,128)}, u32[]{:S(2)}) copy-start(f32[2,40,8,256]{3,2,1,0:T(8,128)} %get-tuple-element.22) | copy-start | bytes 1966084
  138.8 15.4 %copy-start.27 = (f32[2,40,8,256]{3,2,1,0:T(8,128)S(1)}, f32[2,40,8,256]{3,2,1,0:T(8,128)}, u32[]{:S(2)}) copy-start(f32[2,40,8,256]{3,2,1,0:T(8,128)} %get-tuple-element.21) | copy-start | bytes 1966084
  138.8 17.2 %copy-start.24 = (f32[2,40,8,256]{3,2,1,0:T(8,128)S(1)}, f32[2,40,8,256]{3,2,1,0:T(8,128)}, u32[]{:S(2)}) copy-start(f32[2,40,8,256]{3,2,1,0:T(8,128)} %get-tuple-element.20) | copy-start | bytes 1966084
  138.8 18.1 %copy-start.23 = (f32[2,40,8,256]{3,2,1,0:T(8,128)S(1)}, f32[2,40,8,256]{3,2,1,0:T(8,128)}, u32[]{:S(2)}) copy-start(f32[2,40,8,256]{3,2,1,0:T(8,128)} %get-tuple-element.19) | copy-start | bytes 1966084
  138.8 20.0 %copy-start.20 = (f32[2,40,8,256]{3,2,1,0:T(8,128)S(1)}, f32[2,40,8,256]{3,2,1,0:T(8,128)}, u32[]{:S(2)}) copy-start(f32[2,40,8,256]{3,2,1,0:T(8,128)} %get-tuple-element.18) | copy-start | bytes 1966084
  138.9 20.9 %copy-start.19 = (f32[2,40,8,256]{3,2,1,0:T(8,128)S(1)}, f32[2,40,8,256]{3,2,1,0:T(8,128)}, u32[]{:S(2)}) copy-start(f32[2,40,8,256]{3,2,1,0:T(8,128)} %get-tuple-element.17) | copy-start | bytes 1966084
  141.1 20.4 %copy-start.16 = (f32[2,40,8,256]{3,2,1,0:T(8,128)S(1)}, f32[2,40,8,256]{3,2,1,0:T(8,128)}, u32[]{:S(2)}) copy-start(f32[2,40,8,256]{3,2,1,0:T(8,128)} %get-tuple-element.16) | copy-start | bytes 1966084
  141.1 21.3 %copy-start.15 = (f32[2,40,8,256]{3,2,1,0:T(8,128)S(1)}, f32[2,40,8,256]{3,2,1,0:T(8,128)}, u32[]{:S(2)}) copy-start(f32[2,40,8,256]{3,2,1,0:T(8,128)} %get-tuple-element.15) | copy-start | bytes 1966084
  143.1 21.1 %copy-start.12 = (f32[2,40,8,256]{3,2,1,0:T(8,128)S(1)}, f32[2,40,8,256]{3,2,1,0:T(8,128)}, u32[]{:S(2)}) copy-start(f32[2,40,8,256]{3,2,1,0:T(8,128)} %get-tuple-element.14) | copy-start | bytes 1966084
  143.1 22.0 %copy-start.11 = (f32[2,40,8,256]{3,2,1,0:T(8,128)S(1)}, f32[2,40,8,256]{3,2,1,0:T(8,128)}, u32[]{:S(2)}) copy-start(f32[2,40,8,256]{3,2,1,0:T(8,128)} %get-tuple-element.13) | copy-start | bytes 1966084
  143.5 23.4 %copy-start.9 = (f32[2,40,8,256]{3,2,1,0:T(8,128)S(1)}, f32[2,40,8,256]{3,2,1,0:T(8,128)}, u32[]{:S(2)}) copy-start(f32[2,40,8,256]{3,2,1,0:T(8,128)} %get-tuple-element.12) | copy-start | bytes 1966084
  143.5 24.3 %copy-start.8 = (f32[2,40,8,256]{3,2,1,0:T(8,128)S(1)}, f32[2,40,8,256]{3,2,1,0:T(8,128)}, u32[]{:S(2)}) copy-start(f32[2,40,8,256]{3,2,1,0:T(8,128)} %get-tuple-element.11) | copy-start | bytes 1966084
  143.5 26.1 %copy-start.7 = (f32[2,40,8,256]{3,2,1,0:T(8,128)S(1)}, f32[2,40,8,256]{3,2,1,0:T(8,128)}, u32[]{:S(2)}) copy-start(f32[2,40,8,256]{3,2,1,0:T(8,128)} %get-tuple-element.10) | copy-start | bytes 1966084
  144.4 26.1 %slice-start = ((s8[7077888]{0:T(1024)(128)(4,1)}), s8[4194304]{0:T(1024)(128)(4,1)S(1)}, s32[]{:S(2)}) async-start(s8[7077888]{0:T(1024)(128)(4,1)} %bitcast.78), calls=%async_computation.3 | async-start | bytes 8388608
  157.9 12.5 %slice-start.1 = ((s8[7077888]{0:T(1024)(128)(4,1)}), s8[2883584]{0:T(1024)(128)(4,1)S(1)}, s32[]{:S(2)}) async-start(s8[7077888]{0:T(1024)(128)(4,1)} %bitcast.78), calls=%async_computation.4 | async-start | bytes 5767168
  166.0 15.2 %copy-start.34 = (f32[2,40,8,256]{3,2,1,0:T(8,128)S(1)}, f32[2,40,8,256]{3,2,1,0:T(8,128)}, u32[]{:S(2)}) copy-start(f32[2,40,8,256]{3,2,1,0:T(8,128)} %param.9) | copy-start | bytes 1966084
  166.9 32.3 %copy-start.1 = (f32[4,256]{1,0:T(4,128)S(1)}, f32[4,256]{1,0:T(4,128)}, u32[]{:S(2)}) copy-start(f32[4,256]{1,0:T(4,128)} %param.13) | copy-start | bytes 12292
  (3 other events, 2.7 us)
Sparse Core Ops, SparseCore 0:
  10.2 69.3 all-gather.1
  110.7 88.3 reduce-scatter.1
where the time goes:
time: 207 us; the launch traced here: 206 us
  local copies, waits for them, and re-layouts  58.4 us (28%)
  waiting for transfers between devices  54 us (26%)
  matrix products  42.2 us (20%)
  other arithmetic  20.1 us (10%)
  starting transfers between devices  16.6 us (8%)
  between operations  14.8 us (7%)
    unnamed x135, local copies, waits for them, and re-layouts  45.8 us
    all_gather x1, waiting for transfers between devices, per_device(): full_weight = lax.all_gather(weight, 'space', axis=0, tiled=True)  27.6 us
    reduce_scatter x1, waiting for transfers between devices, per_device(): lax.psum_scatter(stacked_product(delta_flat, table_pre), 'space', scatter...  17.1 us
    dot_general x1, matrix products, stacked_product(): jnp.einsum('rq,rop->opq', lhs, rhs, preferred_element_type=jnp.float32)  16.7 us
    dot_general x1, matrix products, conv_piece(): return jnp.einsum('rop,poc->rc', table, piece, precision=high)  13.7 us
    dot_general x1, matrix products, back_piece(): return jnp.einsum('roc,qoc->rq', table, piece, precision=high)  10.7 us
    slice x3, local copies, waits for them, and re-layouts, window_table(): grid[lat_off:lat_off + out_rows, lon_off:lon_off + lon_n, lev_off:lev_off...  9.24 us
    ppermute x4, waiting for transfers between devices, all_sum(): x = x + lax.ppermute(x, 'space', [(i, i ^ bit) for i in range(count)])  8.57 us
  transfers between devices with their start and end apart: 10, of which 5 were waited for; matrix products, arithmetic and copies ran while one was open for 39% of the time, Pallas kernels for 0%

commit v1 on v0

--- a/solution.py
+++ b/solution.py
@@ -81,7 +81,15 @@
         level_index[:, None] == jnp.arange(level_gain.shape[0], dtype=jnp.int32)[None, :]
     ).astype(jnp.float32)
     gains = jnp.dot(one_hot, level_gain, precision=highest)
-    full_weight = lax.all_gather(weight, "space", axis=0, tiled=True)
+    n_chips = lax.axis_size("space")
+    piece_out = weight
+    all_values = [(b - 1, b) for b in range(1, n_chips)] + [(n_chips - 1, 0)]
+    in_order = [piece_out]
+    for _ in range(n_chips - 1):
+        piece_out = lax.ppermute(piece_out, perm=all_values, axis_name="space")
+        in_order += [piece_out]
+    answer = jnp.concatenate([*reversed(in_order)], axis=0)
+    full_weight = jnp.roll(answer, shift=(lax.axis_index("space") + 1) * piece_out.shape[0], axis=0)
     grid_pre = wrap_levels(with_halo(field, (("space", 0),), 1))
     table_pre = window_table(grid_pre, rows, False)
     conv = conv_piece(table_pre, full_weight)

time: 207 us -> 312 us (1.51)
  waiting for transfers between devices: 54 us -> 156 us
  starting transfers between devices: 16.6 us -> 11.7 us
  local copies, waits for them, and re-layouts: 58.4 us -> 61.6 us
    ppermute x0 -> x15, waiting for transfers between devices: none -> 123 us  [per_device(): piece_out = lax.ppermute(piece_out, perm=all_values, axis_name='space')]
    all_gather x1 -> x0, waiting for transfers between devices: 27.6 us -> none  [per_device(): full_weight = lax.all_gather(weight, 'space', axis=0, tiled=True)]
    ppermute x4, starting transfers between devices: 8.5 us -> 2.84 us  [all_sum(): x = x + lax.ppermute(x, 'space', [(i, i ^ bit) for i in range(count)])]
    ppermute x4, waiting for transfers between devices: 8.57 us -> 12.6 us  [all_sum(): x = x + lax.ppermute(x, 'space', [(i, i ^ bit) for i in range(count)])]
    unnamed x135 -> x228, local copies, waits for them, and re-layouts: 45.8 us -> 49.4 us
    reduce_scatter x1, waiting for transfers between devices: 17.1 us -> 20.4 us  [per_device(): lax.psum_scatter(stacked_product(delta_flat, table_pre), 'space', scatter...]
  transfers between devices with their start and end apart: 10 -> 24, of which waited for: 5 -> 19; matrix products, arithmetic and copies ran while one was open for 39% -> 25% of each run, Pallas kernels for 0% -> 0%
where the time goes in v1:
time: 312 us; the launch traced here: 311 us
  waiting for transfers between devices  156 us (50%)
  local copies, waits for them, and re-layouts  61.6 us (20%)
  matrix products  44.5 us (14%)
  other arithmetic  21.7 us (7%)
  between operations  15.3 us (5%)
  starting transfers between devices  11.7 us (4%)
    ppermute x15, waiting for transfers between devices, per_device(): piece_out = lax.ppermute(piece_out, perm=all_values, axis_name='space')  123 us
    unnamed x228, local copies, waits for them, and re-layouts  49.4 us
    reduce_scatter x1, waiting for transfers between devices, per_device(): lax.psum_scatter(stacked_product(delta_flat, table_pre), 'space', scatter...  20.4 us
    dot_general x1, matrix products, stacked_product(): jnp.einsum('rq,rop->opq', lhs, rhs, preferred_element_type=jnp.float32)  16.2 us
    dot_general x1, matrix products, conv_piece(): return jnp.einsum('rop,poc->rc', table, piece, precision=high)  15.8 us
    ppermute x4, waiting for transfers between devices, all_sum(): x = x + lax.ppermute(x, 'space', [(i, i ^ bit) for i in range(count)])  12.6 us
    dot_general x1, matrix products, back_piece(): return jnp.einsum('roc,qoc->rq', table, piece, precision=high)  11.5 us
    slice x3, local copies, waits for them, and re-layouts, window_table(): grid[lat_off:lat_off + out_rows, lon_off:lon_off + lon_n, lev_off:lev_off...  8.92 us
  transfers between devices with their start and end apart: 24, of which 19 were waited for; matrix products, arithmetic and copies ran while one was open for 25% of the time, Pallas kernels for 0%

profile of v1, /device:TPU:0, one launch (start us, length us, event | category | flops | bytes accessed | tf_op | source)
XLA Modules:
  0.0 311.3 jit_solution(8129849673148904378)
XLA Ops:
  7.7 11.2 %collective-permute-done.2 = f32[16,27,256]{2,0,1:T(8,128)S(1)} collective-permute-done((f32[16,27,256]{2,0,1:T(8,128)}, f32[16,27,256]{2,0,1:T(8,128)S(1)}, u32[]{:S(2)}, u32[]{:S(2)}) %collective-permute-start.2) | collective-permute-done | bytes 442400 | tf_op jit(solution)/shard_map/ppermute | solution.py:89
  19.7 10.4 %collective-permute-done.3 = f32[16,27,256]{2,0,1:T(8,128)S(1)} collective-permute-done((f32[16,27,256]{2,0,1:T(8,128)S(1)}, f32[16,27,256]{2,0,1:T(8,128)S(1)}, u32[]{:S(2)}, u32[]{:S(2)}) %collective-permute-start.3) | collective-permute-done | bytes 442400 | tf_op jit(solution)/shard_map/ppermute | solution.py:89
  30.9 10.4 %collective-permute-done.4 = f32[16,27,256]{2,0,1:T(8,128)S(1)} collective-permute-done((f32[16,27,256]{2,0,1:T(8,128)S(1)}, f32[16,27,256]{2,0,1:T(8,128)S(1)}, u32[]{:S(2)}, u32[]{:S(2)}) %collective-permute-start.4) | collective-permute-done | bytes 442400 | tf_op jit(solution)/shard_map/ppermute | solution.py:89
  42.1 1.1 fusion.36
  43.2 1.3 collective-permute-start.1
  44.5 3.1 collective-permute-start
  48.3 1.4 broadcast_multiply_fusion
  49.7 2.9 collective-permute-done.5
  53.4 2.5 pad_maximum_fusion.4
  56.0 6.9 %collective-permute-done.6 = f32[16,27,256]{2,0,1:T(8,128)S(1)} collective-permute-done((f32[16,27,256]{2,0,1:T(8,128)S(1)}, f32[16,27,256]{2,0,1:T(8,128)S(1)}, u32[]{:S(2)}, u32[]{:S(2)}) %collective-permute-start.6) | collective-permute-done | bytes 442400 | tf_op jit(solution)/shard_map/ppermute | solution.py:89
  63.4 10.0 %collective-permute-done.7 = f32[16,27,256]{2,0,1:T(8,128)} collective-permute-done((f32[16,27,256]{2,0,1:T(8,128)S(1)}, f32[16,27,256]{2,0,1:T(8,128)}, u32[]{:S(2)}, u32[]{:S(2)}) %collective-permute-start.7) | collective-permute-done | bytes 442400 | tf_op jit(solution)/shard_map/ppermute | solution.py:89
  73.5 4.2 %fusion.31 = (f32[2,40,8,256]{3,2,1,0:T(8,128)S(1)}, f32[2,40,8,256]{3,2,1,0:T(8,128)}, f32[2,40,8,256]{3,2,1,0:T(8,128)}, f32[2,40,8,256]{3,2,1,0:T(8,128)}, f3...) fusion(f32[4,42,10,256]{3,2,1,0:T(8,128)S(1)} %select_maximum_f, ...), kind=kLoop, calls=%fused_computation.160 | loop fusion | bytes 23592960 | tf_op jit(solution)/shard_map/slice | solution.py:38
  77.7 1.3 constant_dynamic-update-slice_fusion.29
  79.0 5.2 %collective-permute-done.8 = f32[16,27,256]{2,0,1:T(8,128)} collective-permute-done((f32[16,27,256]{2,0,1:T(8,128)}, f32[16,27,256]{2,0,1:T(8,128)}, u32[]{:S(2)}, u32[]{:S(2)}) %collective-permute-start.8) | collective-permute-done | bytes 442400 | tf_op jit(solution)/shard_map/ppermute | solution.py:89
  84.2 2.5 pad_maximum_fusion.3
  86.8 1.3 constant_dynamic-update-slice_fusion.27
  88.1 6.8 %collective-permute-done.9 = f32[16,27,256]{2,0,1:T(8,128)S(1)} collective-permute-done((f32[16,27,256]{2,0,1:T(8,128)}, f32[16,27,256]{2,0,1:T(8,128)S(1)}, u32[]{:S(2)}, u32[]{:S(2)}) %collective-permute-start.9) | collective-permute-done | bytes 442400 | tf_op jit(solution)/shard_map/ppermute | solution.py:89
  94.9 1.3 constant_dynamic-update-slice_fusion.26
  96.2 1.1 constant_dynamic-update-slice_fusion.25
  97.3 1.1 constant_dynamic-update-slice_fusion.24
  98.4 1.1 constant_dynamic-update-slice_fusion.23
  99.6 5.7 %collective-permute-done.10 = f32[16,27,256]{2,0,1:T(8,128)S(1)} collective-permute-done((f32[16,27,256]{2,0,1:T(8,128)S(1)}, f32[16,27,256]{2,0,1:T(8,128)S(1)}, u32[]{:S(2)}, u32[]{:S(2)}) %collective-permute-start.10) | collective-permute-done | bytes 442400 | tf_op jit(solution)/shard_map/ppermute | solution.py:89
  105.5 10.2 %collective-permute-done.11 = f32[16,27,256]{2,0,1:T(8,128)S(1)} collective-permute-done((f32[16,27,256]{2,0,1:T(8,128)S(1)}, f32[16,27,256]{2,0,1:T(8,128)S(1)}, u32[]{:S(2)}, u32[]{:S(2)}) %collective-permute-start.11) | collective-permute-done | bytes 442400 | tf_op jit(solution)/shard_map/ppermute | solution.py:89
  116.0 10.2 %collective-permute-done.12 = f32[16,27,256]{2,0,1:T(8,128)S(1)} collective-permute-done((f32[16,27,256]{2,0,1:T(8,128)S(1)}, f32[16,27,256]{2,0,1:T(8,128)S(1)}, u32[]{:S(2)}, u32[]{:S(2)}) %collective-permute-start.12) | collective-permute-done | bytes 442400 | tf_op jit(solution)/shard_map/ppermute | solution.py:89
  126.4 10.2 %collective-permute-done.13 = f32[16,27,256]{2,0,1:T(8,128)S(1)} collective-permute-done((f32[16,27,256]{2,0,1:T(8,128)S(1)}, f32[16,27,256]{2,0,1:T(8,128)S(1)}, u32[]{:S(2)}, u32[]{:S(2)}) %collective-permute-start.13) | collective-permute-done | bytes 442400 | tf_op jit(solution)/shard_map/ppermute | solution.py:89
  136.8 10.2 %collective-permute-done.14 = f32[16,27,256]{2,0,1:T(8,128)S(1)} collective-permute-done((f32[16,27,256]{2,0,1:T(8,128)S(1)}, f32[16,27,256]{2,0,1:T(8,128)S(1)}, u32[]{:S(2)}, u32[]{:S(2)}) %collective-permute-start.14) | collective-permute-done | bytes 442400 | tf_op jit(solution)/shard_map/ppermute | solution.py:89
  147.3 10.1 %collective-permute-done.15 = f32[16,27,256]{2,0,1:T(8,128)S(1)} collective-permute-done((f32[16,27,256]{2,0,1:T(8,128)S(1)}, f32[16,27,256]{2,0,1:T(8,128)S(1)}, u32[]{:S(2)}, u32[]{:S(2)}) %collective-permute-start.15) | collective-permute-done | bytes 442400 | tf_op jit(solution)/shard_map/ppermute | solution.py:89
  157.4 7.4 %fusion.6 = (bf16[640,27,256]{2,0,1:T(8,128)(2,1)}, bf16[640,27,256]{2,0,1:T(8,128)(2,1)}) fusion(f32[640,27,256]{2,0,1:T(8,128)S(1)} %constant_dynamic-update-slice_fusion.3), kind=kLoop, calls=%fused_computation.8 | loop fusion | flops 17694720 | bytes 35389440 | tf_op jit(solution)/shard_map/convert_element_type | solution.py:74
  164.9 3.0 collective-permute-done.16
  168.0 1.1 constant_dynamic-update-slice_fusion.61
  169.1 1.0 constant_dynamic-update-slice_fusion.60
  170.2 1.0 constant_dynamic-update-slice_fusion.59
  171.2 1.0 constant_dynamic-update-slice_fusion.58
  181.6 15.8 %fusion.9 = f32[640,256,1]{1,0,2:T(8,128)} fusion(f32[640,27,256]{2,0,1:T(8,128)} %copy-done.2, f32[512,27,256]{2,0,1:T(8,128)S(1)} %constant_dynamic-update-slice_fusion.30, s32[]{:T(128)S(6)} %select_n.14), kind=kOutput, calls=%fused_computation.11 | convolution fusion | flops 6794772480 | bytes 25427972 | tf_op jit(solution)/shard_map/rop,poc->rc/dot_general | solution.py:46
  197.4 1.7 fusion.29
  199.2 16.2 %fusion = f32[27,256,256]{2,1,0:T(8,128)} fusion(bf16[640,27,256]{2,0,1:T(8,128)(2,1)} %get-tuple-element.9, bf16[640,27,256]{2,0,1:T(8,128)(2,1)} %get-tuple-element.8, bf16[640,256]{1,0:T(8,128)(2,1)S(1)} %get-tuple-element.69, bf16[640,256]{1,0:T(8,128)(2,1)S(1)} %get-tuple-element.68), kind=kOutput, calls=%fused_computation | convolution fusion | flops 6877347840 | bytes 25427968 | tf_op jit(solution)/shard_map/rq,rop->opq/dot_general | solution.py:58
  215.9 2.4 collective-permute-start.17
  218.3 1.5 collective-permute-start.18
  219.8 2.3 collective-permute-start.20
  222.1 4.9 %collective-permute-done.20 = f32[6,256]{1,0:T(8,128)S(1)} collective-permute-done((f32[6,256]{1,0:T(8,128)S(1)}, f32[6,256]{1,0:T(8,128)S(1)}, u32[]{:S(2)}, u32[]{:S(2)}) %collective-permute-start.20) | collective-permute-done | bytes 6176 | tf_op jit(solution)/shard_map/ppermute | solution.py:67
  227.0 3.6 %collective-permute-done.21 = f32[6,256]{1,0:T(8,128)S(1)} collective-permute-done((f32[6,256]{1,0:T(8,128)S(1)}, f32[6,256]{1,0:T(8,128)S(1)}, u32[]{:S(2)}, u32[]{:S(2)}) %collective-permute-start.21) | collective-permute-done | bytes 6176 | tf_op jit(solution)/shard_map/ppermute | solution.py:67
  231.1 4.1 %collective-permute-done.22 = f32[6,256]{1,0:T(8,128)S(1)} collective-permute-done((f32[6,256]{1,0:T(8,128)S(1)}, f32[6,256]{1,0:T(8,128)S(1)}, u32[]{:S(2)}, u32[]{:S(2)}) %collective-permute-start.22) | collective-permute-done | bytes 6176 | tf_op jit(solution)/shard_map/ppermute | solution.py:67
  237.8 4.4 %fusion.30 = (f32[2,40,8,256]{3,2,1,0:T(8,128)}, f32[2,40,8,256]{3,2,1,0:T(8,128)}, f32[2,40,8,256]{3,2,1,0:T(8,128)}, f32[2,40,8,256]{3,2,1,0:T(8,128)}, f32[2,...) fusion(f32[4,42,10,256]{3,2,1,0:T(8,128)S(1)} %select_maximum_f, ...), kind=kLoop, calls=%fused_computation.159 | loop fusion | bytes 23592960 | tf_op jit(solution)/shard_map/slice | solution.py:38
  242.3 2.1 constant_dynamic-update-slice_fusion.88
  244.5 2.0 maximum_maximum_fusion
  270.3 11.5 %fusion.7 = f32[640,256,1]{1,0,2:T(8,128)} fusion(f32[640,27,256]{2,0,1:T(8,128)} %constant_dynamic-update-slice_fusion.62, f32[512,27,256]{2,0,1:T(8,128)S(1)} %bitcast.77, s32[]{:T(128)S(6)} %select_n.14), kind=kOutput, calls=%fused_computation.9 | convolution fusion | flops 6794772480 | bytes 25427972 | tf_op jit(solution)/shard_map/roc,qoc->rq/dot_general | solution.py:50
  281.8 2.2 add.65
  284.0 20.4 %reduce-scatter.2.cloned.1.call-done = f32[27,16,256]{2,1,0:T(8,128)} async-done(((f32[27,256,256]{2,1,0:T(8,128)}), f32[27,16,256]{2,1,0:T(8,128)}) %reduce-scatter.2.cloned.1.call-update) | async-done | bytes 442384 | tf_op jit(solution)/shard_map/reduce_scatter | solution.py:111
  (265 shorter events, 42.4 us)
Async XLA Ops:
  7.2 45.4 %copy-start = (f32[4,256]{1,0:T(4,128)S(1)}, f32[4,256]{1,0:T(4,128)}, u32[]{:S(2)}) copy-start(f32[4,256]{1,0:T(4,128)} %param.13) | copy-start | bytes 12292
  7.2 297.2 %reduce-scatter.2.cloned.1.call-start = ((), (), s32[]{:S(2)}) async-start(), calls=%async_computation.1 | async-start | bytes 7520256 | tf_op jit(solution)/shard_map/reduce_scatter | solution.py:111
  7.2 11.7 %collective-permute-start.2 = (f32[16,27,256]{2,0,1:T(8,128)}, f32[16,27,256]{2,0,1:T(8,128)S(1)}, u32[]{:S(2)}, u32[]{:S(2)}) collective-permute-start(f32[16,27,256]{2,0,1:T(8,128)} %param.10), channel_id=1, source_target_pairs={{0,1},{1,2},{2,3},{3,4},{4,5},{5,6},{6,7},{7,8},{8,9},{9,10},{10,1... | collective-permute-start | bytes 1327112 | tf_op jit(solution)/shard_map/ppermute | solution.py:89
  19.7 10.4 %collective-permute-start.3 = (f32[16,27,256]{2,0,1:T(8,128)S(1)}, f32[16,27,256]{2,0,1:T(8,128)S(1)}, u32[]{:S(2)}, u32[]{:S(2)}) collective-permute-start(f32[16,27,256]{2,0,1:T(8,128)S(1)} %collective-permute-done.2), channel_id=1, source_target_pairs={{0,1},{1,2},{2,3},{3,4},{4,5},{5,6},{6,7},{7,8},{8,9},{9,10},{10,1... | collective-permute-start | bytes 1327112 | tf_op jit(solution)/shard_map/ppermute | solution.py:89
  30.9 10.4 %collective-permute-start.4 = (f32[16,27,256]{2,0,1:T(8,128)S(1)}, f32[16,27,256]{2,0,1:T(8,128)S(1)}, u32[]{:S(2)}, u32[]{:S(2)}) collective-permute-start(f32[16,27,256]{2,0,1:T(8,128)S(1)} %collective-permute-done.3), channel_id=1, source_target_pairs={{0,1},{1,2},{2,3},{3,4},{4,5},{5,6},{6,7},{7,8},{8,9},{9,10},{10,1... | collective-permute-start | bytes 1327112 | tf_op jit(solution)/shard_map/ppermute | solution.py:89
  42.1 10.4 %collective-permute-start.5 = (f32[16,27,256]{2,0,1:T(8,128)S(1)}, f32[16,27,256]{2,0,1:T(8,128)S(1)}, u32[]{:S(2)}, u32[]{:S(2)}) collective-permute-start(f32[16,27,256]{2,0,1:T(8,128)S(1)} %collective-permute-done.4), channel_id=1, source_target_pairs={{0,1},{1,2},{2,3},{3,4},{4,5},{5,6},{6,7},{7,8},{8,9},{9,10},{10,1... | collective-permute-start | bytes 1327112 | tf_op jit(solution)/shard_map/ppermute | solution.py:89
  43.2 10.2 %collective-permute-start.1 = (f32[1,40,8,256]{3,2,1,0:T(8,128)S(1)}, f32[1,40,8,256]{3,2,1,0:T(8,128)S(1)}, u32[]{:S(2)}, u32[]{:S(2)}) collective-permute-start(f32[1,40,8,256]{3,2,1,0:T(8,128)S(1)} %get-tuple-element.77), channel_id=1, source_target_pairs={{1,0},{2,1},{3,2},{4,3},{5,4},{6,5},{7,6},{8,7},{9,8},{10,9},{11,1... | collective-permute-start | bytes 983048 | tf_op jit(solution)/shard_map/ppermute | solution.py:18
  44.5 8.9 %collective-permute-start = (f32[1,40,8,256]{3,2,1,0:T(8,128)S(1)}, f32[1,40,8,256]{3,2,1,0:T(8,128)S(1)}, u32[]{:S(2)}, u32[]{:S(2)}) collective-permute-start(f32[1,40,8,256]{3,2,1,0:T(8,128)S(1)} %get-tuple-element.78), channel_id=1, source_target_pairs={{0,1},{1,2},{2,3},{3,4},{4,5},{5,6},{6,7},{7,8},{8,9},{9,10},{10,1... | collective-permute-start | bytes 983048 | tf_op jit(solution)/shard_map/ppermute | solution.py:17
  52.5 10.4 %collective-permute-start.6 = (f32[16,27,256]{2,0,1:T(8,128)S(1)}, f32[16,27,256]{2,0,1:T(8,128)S(1)}, u32[]{:S(2)}, u32[]{:S(2)}) collective-permute-start(f32[16,27,256]{2,0,1:T(8,128)S(1)} %collective-permute-done.5), channel_id=1, source_target_pairs={{0,1},{1,2},{2,3},{3,4},{4,5},{5,6},{6,7},{7,8},{8,9},{9,10},{10,1... | collective-permute-start | bytes 1327112 | tf_op jit(solution)/shard_map/ppermute | solution.py:89
  63.0 10.5 %collective-permute-start.7 = (f32[16,27,256]{2,0,1:T(8,128)S(1)}, f32[16,27,256]{2,0,1:T(8,128)}, u32[]{:S(2)}, u32[]{:S(2)}) collective-permute-start(f32[16,27,256]{2,0,1:T(8,128)S(1)} %collective-permute-done.6), channel_id=1, source_target_pairs={{0,1},{1,2},{2,3},{3,4},{4,5},{5,6},{6,7},{7,8},{8,9},{9,10},{10,1... | collective-permute-start | bytes 1327112 | tf_op jit(solution)/shard_map/ppermute | solution.py:89
  73.5 10.7 %collective-permute-start.8 = (f32[16,27,256]{2,0,1:T(8,128)}, f32[16,27,256]{2,0,1:T(8,128)}, u32[]{:S(2)}, u32[]{:S(2)}) collective-permute-start(f32[16,27,256]{2,0,1:T(8,128)} %collective-permute-done.7), channel_id=1, source_target_pairs={{0,1},{1,2},{2,3},{3,4},{4,5},{5,6},{6,7},{7,8},{8,9},{9,10},{10,1... | collective-permute-start | bytes 1327112 | tf_op jit(solution)/shard_map/ppermute | solution.py:89
  77.7 38.1 %copy-start.24 = (f32[2,40,8,256]{3,2,1,0:T(8,128)S(1)}, f32[2,40,8,256]{3,2,1,0:T(8,128)}, u32[]{:S(2)}) copy-start(f32[2,40,8,256]{3,2,1,0:T(8,128)} %get-tuple-element.38) | copy-start | bytes 1966084
  77.7 38.1 %copy-start.23 = (f32[2,40,8,256]{3,2,1,0:T(8,128)S(1)}, f32[2,40,8,256]{3,2,1,0:T(8,128)}, u32[]{:S(2)}) copy-start(f32[2,40,8,256]{3,2,1,0:T(8,128)} %get-tuple-element.37) | copy-start | bytes 1966084
  77.7 38.2 %copy-start.5 = (f32[2,40,8,256]{3,2,1,0:T(8,128)S(1)}, f32[2,40,8,256]{3,2,1,0:T(8,128)}, u32[]{:S(2)}) copy-start(f32[2,40,8,256]{3,2,1,0:T(8,128)} %param.8) | copy-start | bytes 1966084
  77.7 38.2 %copy-start.20 = (f32[2,40,8,256]{3,2,1,0:T(8,128)S(1)}, f32[2,40,8,256]{3,2,1,0:T(8,128)}, u32[]{:S(2)}) copy-start(f32[2,40,8,256]{3,2,1,0:T(8,128)} %get-tuple-element.36) | copy-start | bytes 1966084
  77.7 48.5 %copy-start.17 = (f32[2,40,8,256]{3,2,1,0:T(8,128)S(1)}, f32[2,40,8,256]{3,2,1,0:T(8,128)}, u32[]{:S(2)}) copy-start(f32[2,40,8,256]{3,2,1,0:T(8,128)} %get-tuple-element.35) | copy-start | bytes 1966084
  77.7 48.6 %copy-start.15 = (f32[2,40,8,256]{3,2,1,0:T(8,128)S(1)}, f32[2,40,8,256]{3,2,1,0:T(8,128)}, u32[]{:S(2)}) copy-start(f32[2,40,8,256]{3,2,1,0:T(8,128)} %get-tuple-element.34) | copy-start | bytes 1966084
  79.0 47.3 %copy-start.14 = (f32[2,40,8,256]{3,2,1,0:T(8,128)S(1)}, f32[2,40,8,256]{3,2,1,0:T(8,128)}, u32[]{:S(2)}) copy-start(f32[2,40,8,256]{3,2,1,0:T(8,128)} %get-tuple-element.33) | copy-start | bytes 1966084
  79.0 57.6 %copy-start.13 = (f32[2,40,8,256]{3,2,1,0:T(8,128)S(1)}, f32[2,40,8,256]{3,2,1,0:T(8,128)}, u32[]{:S(2)}) copy-start(f32[2,40,8,256]{3,2,1,0:T(8,128)} %get-tuple-element.32) | copy-start | bytes 1966084
  84.2 10.6 %collective-permute-start.9 = (f32[16,27,256]{2,0,1:T(8,128)}, f32[16,27,256]{2,0,1:T(8,128)S(1)}, u32[]{:S(2)}, u32[]{:S(2)}) collective-permute-start(f32[16,27,256]{2,0,1:T(8,128)} %collective-permute-done.8), channel_id=1, source_target_pairs={{0,1},{1,2},{2,3},{3,4},{4,5},{5,6},{6,7},{7,8},{8,9},{9,10},{10,1... | collective-permute-start | bytes 1327112 | tf_op jit(solution)/shard_map/ppermute | solution.py:89
  86.7 50.0 %copy-start.12 = (f32[2,40,8,256]{3,2,1,0:T(8,128)S(1)}, f32[2,40,8,256]{3,2,1,0:T(8,128)}, u32[]{:S(2)}) copy-start(f32[2,40,8,256]{3,2,1,0:T(8,128)} %get-tuple-element.31) | copy-start | bytes 1966084
  86.7 50.0 %copy-start.39 = (f32[2,40,8,256]{3,2,1,0:T(8,128)S(1)}, f32[2,40,8,256]{3,2,1,0:T(8,128)}, u32[]{:S(2)}) copy-start(f32[2,40,8,256]{3,2,1,0:T(8,128)} %get-tuple-element.74) | copy-start | bytes 1966084
  86.8 60.3 %copy-start.11 = (f32[2,40,8,256]{3,2,1,0:T(8,128)S(1)}, f32[2,40,8,256]{3,2,1,0:T(8,128)}, u32[]{:S(2)}) copy-start(f32[2,40,8,256]{3,2,1,0:T(8,128)} %get-tuple-element.30) | copy-start | bytes 1966084
  86.8 60.3 %copy-start.10 = (f32[2,40,8,256]{3,2,1,0:T(8,128)S(1)}, f32[2,40,8,256]{3,2,1,0:T(8,128)}, u32[]{:S(2)}) copy-start(f32[2,40,8,256]{3,2,1,0:T(8,128)} %get-tuple-element.29) | copy-start | bytes 1966084
  94.9 52.3 %copy-start.51 = (f32[16,27,256]{2,0,1:T(8,128)}, f32[16,27,256]{2,0,1:T(8,128)S(1)}, u32[]{:S(2)}) copy-start(f32[16,27,256]{2,0,1:T(8,128)S(1)} %collective-permute-done.9) | copy-start | bytes 1327108
  94.9 10.4 %collective-permute-start.10 = (f32[16,27,256]{2,0,1:T(8,128)S(1)}, f32[16,27,256]{2,0,1:T(8,128)S(1)}, u32[]{:S(2)}, u32[]{:S(2)}) collective-permute-start(f32[16,27,256]{2,0,1:T(8,128)S(1)} %collective-permute-done.9), channel_id=1, source_target_pairs={{0,1},{1,2},{2,3},{3,4},{4,5},{5,6},{6,7},{7,8},{8,9},{9,10},{10,1... | collective-permute-start | bytes 1327112 | tf_op jit(solution)/shard_map/ppermute | solution.py:89
  105.3 59.6 %copy-start.53 = (f32[16,27,256]{2,0,1:T(8,128)}, f32[16,27,256]{2,0,1:T(8,128)S(1)}, u32[]{:S(2)}) copy-start(f32[16,27,256]{2,0,1:T(8,128)S(1)} %collective-permute-done.10) | copy-start | bytes 1327108
  105.3 10.4 %collective-permute-start.11 = (f32[16,27,256]{2,0,1:T(8,128)S(1)}, f32[16,27,256]{2,0,1:T(8,128)S(1)}, u32[]{:S(2)}, u32[]{:S(2)}) collective-permute-start(f32[16,27,256]{2,0,1:T(8,128)S(1)} %collective-permute-done.10), channel_id=1, source_target_pairs={{0,1},{1,2},{2,3},{3,4},{4,5},{5,6},{6,7},{7,8},{8,9},{9,10},{10,1... | collective-permute-start | bytes 1327112 | tf_op jit(solution)/shard_map/ppermute | solution.py:89
  115.7 49.2 %copy-start.55 = (f32[16,27,256]{2,0,1:T(8,128)}, f32[16,27,256]{2,0,1:T(8,128)S(1)}, u32[]{:S(2)}) copy-start(f32[16,27,256]{2,0,1:T(8,128)S(1)} %collective-permute-done.11) | copy-start | bytes 1327108
  115.7 10.4 %collective-permute-start.12 = (f32[16,27,256]{2,0,1:T(8,128)S(1)}, f32[16,27,256]{2,0,1:T(8,128)S(1)}, u32[]{:S(2)}, u32[]{:S(2)}) collective-permute-start(f32[16,27,256]{2,0,1:T(8,128)S(1)} %collective-permute-done.11), channel_id=1, source_target_pairs={{0,1},{1,2},{2,3},{3,4},{4,5},{5,6},{6,7},{7,8},{8,9},{9,10},{10,1... | collective-permute-start | bytes 1327112 | tf_op jit(solution)/shard_map/ppermute | solution.py:89
  126.1 10.4 %collective-permute-start.13 = (f32[16,27,256]{2,0,1:T(8,128)S(1)}, f32[16,27,256]{2,0,1:T(8,128)S(1)}, u32[]{:S(2)}, u32[]{:S(2)}) collective-permute-start(f32[16,27,256]{2,0,1:T(8,128)S(1)} %collective-permute-done.12), channel_id=1, source_target_pairs={{0,1},{1,2},{2,3},{3,4},{4,5},{5,6},{6,7},{7,8},{8,9},{9,10},{10,1... | collective-permute-start | bytes 1327112 | tf_op jit(solution)/shard_map/ppermute | solution.py:89
  136.6 10.4 %collective-permute-start.14 = (f32[16,27,256]{2,0,1:T(8,128)S(1)}, f32[16,27,256]{2,0,1:T(8,128)S(1)}, u32[]{:S(2)}, u32[]{:S(2)}) collective-permute-start(f32[16,27,256]{2,0,1:T(8,128)S(1)} %collective-permute-done.13), channel_id=1, source_target_pairs={{0,1},{1,2},{2,3},{3,4},{4,5},{5,6},{6,7},{7,8},{8,9},{9,10},{10,1... | collective-permute-start | bytes 1327112 | tf_op jit(solution)/shard_map/ppermute | solution.py:89
  147.0 10.4 %collective-permute-start.15 = (f32[16,27,256]{2,0,1:T(8,128)S(1)}, f32[16,27,256]{2,0,1:T(8,128)S(1)}, u32[]{:S(2)}, u32[]{:S(2)}) collective-permute-start(f32[16,27,256]{2,0,1:T(8,128)S(1)} %collective-permute-done.14), channel_id=1, source_target_pairs={{0,1},{1,2},{2,3},{3,4},{4,5},{5,6},{6,7},{7,8},{8,9},{9,10},{10,1... | collective-permute-start | bytes 1327112 | tf_op jit(solution)/shard_map/ppermute | solution.py:89
  147.3 28.2 %copy-start.52 = (f32[16,27,256]{2,0,1:T(8,128)S(1)}, f32[16,27,256]{2,0,1:T(8,128)}, u32[]{:S(2)}) copy-start(f32[16,27,256]{2,0,1:T(8,128)} %copy-done.51) | copy-start | bytes 1327108
  147.3 30.3 %copy-start.50 = (f32[16,27,256]{2,0,1:T(8,128)S(1)}, f32[16,27,256]{2,0,1:T(8,128)}, u32[]{:S(2)}) copy-start(f32[16,27,256]{2,0,1:T(8,128)} %copy-done.49) | copy-start | bytes 1327108
  147.3 30.3 %copy-start.48 = (f32[16,27,256]{2,0,1:T(8,128)S(1)}, f32[16,27,256]{2,0,1:T(8,128)}, u32[]{:S(2)}) copy-start(f32[16,27,256]{2,0,1:T(8,128)} %copy-done.47) | copy-start | bytes 1327108
  147.3 30.4 %copy-start.46 = (f32[16,27,256]{2,0,1:T(8,128)S(1)}, f32[16,27,256]{2,0,1:T(8,128)}, u32[]{:S(2)}) copy-start(f32[16,27,256]{2,0,1:T(8,128)} %copy-done.45) | copy-start | bytes 1327108
  147.3 30.4 %copy-start.44 = (f32[16,27,256]{2,0,1:T(8,128)S(1)}, f32[16,27,256]{2,0,1:T(8,128)}, u32[]{:S(2)}) copy-start(f32[16,27,256]{2,0,1:T(8,128)} %copy-done.43) | copy-start | bytes 1327108
  147.3 30.5 %copy-start.42 = (f32[16,27,256]{2,0,1:T(8,128)S(1)}, f32[16,27,256]{2,0,1:T(8,128)}, u32[]{:S(2)}) copy-start(f32[16,27,256]{2,0,1:T(8,128)} %copy-done.41) | copy-start | bytes 1327108
  147.3 30.5 %copy-start.40 = (f32[16,27,256]{2,0,1:T(8,128)S(1)}, f32[16,27,256]{2,0,1:T(8,128)}, u32[]{:S(2)}) copy-start(f32[16,27,256]{2,0,1:T(8,128)} %param.10) | copy-start | bytes 1327108
  157.4 10.5 %collective-permute-start.16 = (f32[16,27,256]{2,0,1:T(8,128)S(1)}, f32[16,27,256]{2,0,1:T(8,128)}, u32[]{:S(2)}, u32[]{:S(2)}) collective-permute-start(f32[16,27,256]{2,0,1:T(8,128)S(1)} %collective-permute-done.15), channel_id=1, source_target_pairs={{0,1},{1,2},{2,3},{3,4},{4,5},{5,6},{6,7},{7,8},{8,9},{9,10},{10,1... | collective-permute-start | bytes 1327112 | tf_op jit(solution)/shard_map/ppermute | solution.py:89
  215.7 4.1 %collective-permute-start.19 = (f32[6,256]{1,0:T(8,128)S(1)}, f32[6,256]{1,0:T(8,128)S(1)}, u32[]{:S(2)}, u32[]{:S(2)}) collective-permute-start(f32[6,256]{1,0:T(8,128)S(1)} %pad_maximum_fusion.10), channel_id=1, source_target_pairs={{0,1},{1,0},{2,3},{3,2},{4,5},{5,4},{6,7},{7,6},{8,9},{9,8},{10,11... | collective-permute-start | bytes 18440 | tf_op jit(solution)/shard_map/ppermute | solution.py:67
  215.9 20.6 %collective-permute-start.17 = (f32[1,40,8,256]{3,2,1,0:T(8,128)S(1)}, f32[1,40,8,256]{3,2,1,0:T(8,128)S(1)}, u32[]{:S(2)}, u32[]{:S(2)}) collective-permute-start(f32[1,40,8,256]{3,2,1,0:T(8,128)S(1)} %get-tuple-element.72), channel_id=1, source_target_pairs={{0,1},{1,2},{2,3},{3,4},{4,5},{5,6},{6,7},{7,8},{8,9},{9,10},{10,1... | collective-permute-start | bytes 983048 | tf_op jit(solution)/shard_map/ppermute | solution.py:17
  218.3 18.1 %collective-permute-start.18 = (f32[1,40,8,256]{3,2,1,0:T(8,128)S(1)}, f32[1,40,8,256]{3,2,1,0:T(8,128)S(1)}, u32[]{:S(2)}, u32[]{:S(2)}) collective-permute-start(f32[1,40,8,256]{3,2,1,0:T(8,128)S(1)} %get-tuple-element.73), channel_id=1, source_target_pairs={{1,0},{2,1},{3,2},{4,3},{5,4},{6,5},{7,6},{8,7},{9,8},{10,9},{11,1... | collective-permute-start | bytes 983048 | tf_op jit(solution)/shard_map/ppermute | solution.py:18
  219.8 7.2 %collective-permute-start.20 = (f32[6,256]{1,0:T(8,128)S(1)}, f32[6,256]{1,0:T(8,128)S(1)}, u32[]{:S(2)}, u32[]{:S(2)}) collective-permute-start(f32[6,256]{1,0:T(8,128)S(1)} %fusion.28), channel_id=1, source_target_pairs={{0,2},{1,3},{2,0},{3,1},{4,6},{5,7},{6,4},{7,5},{8,10},{9,11},{10,... | collective-permute-start | bytes 18440 | tf_op jit(solution)/shard_map/ppermute | solution.py:67
  227.0 3.7 %collective-permute-start.21 = (f32[6,256]{1,0:T(8,128)S(1)}, f32[6,256]{1,0:T(8,128)S(1)}, u32[]{:S(2)}, u32[]{:S(2)}) collective-permute-start(f32[6,256]{1,0:T(8,128)S(1)} %add.67), channel_id=1, source_target_pairs={{0,4},{1,5},{2,6},{3,7},{4,0},{5,1},{6,2},{7,3},{8,12},{9,13},{10,... | collective-permute-start | bytes 18440 | tf_op jit(solution)/shard_map/ppermute | solution.py:67
  230.7 4.5 %collective-permute-start.22 = (f32[6,256]{1,0:T(8,128)S(1)}, f32[6,256]{1,0:T(8,128)S(1)}, u32[]{:S(2)}, u32[]{:S(2)}) collective-permute-start(f32[6,256]{1,0:T(8,128)S(1)} %add.68), channel_id=1, source_target_pairs={{0,8},{1,9},{2,10},{3,11},{4,12},{5,13},{6,14},{7,15},{8,0},{9,1},... | collective-permute-start | bytes 18440 | tf_op jit(solution)/shard_map/ppermute | solution.py:67
  269.4 35.0 %copy-start.1 = (f32[4,256]{1,0:T(4,128)S(1)}, f32[4,256]{1,0:T(4,128)}, u32[]{:S(2)}) copy-start(f32[4,256]{1,0:T(4,128)} %param.13) | copy-start | bytes 12292
  (48 other events, 584.1 us)
Sparse Core Ops, SparseCore 0:
  215.6 88.8 reduce-scatter.1
